TPU v7x, 256 devices: a whole 4x4x8 slice. The times are simulated.
256 devices in a mesh: space: 64 (over x, y, z_hi), chan: 4 (over z_lo, core).
Axes of the slice: x: 4, y: 4, z: 8 (z_hi: 4, z_lo: 2; z = z_hi * 2 + z_lo), core: 2. Of those that a mesh axis runs over, the one named last changes fastest.
Arguments:
- voxels: bfloat16 [32, 128, 16, 512], P(None, 'space'), may hold values from -6 to 6
- first_filters: bfloat16 [3, 3, 3, 64, 32], P(None, None, None, 'chan'), may hold values from -0.21875 to 0.21875
- second_filters: bfloat16 [3, 3, 3, 64, 64], P(None, None, None, 'chan'), may hold values from -0.15625 to 0.15625
Outputs:
- filtered: bfloat16 [64, 128, 16, 512], P('chan', 'space')
All inputs are finite; a program needn't handle non-finite values.
Results may differ from a plain program's by a relative error of at most 0.0049.
Values may be sent and summed in bfloat16 or wider, within the bound.
No kernel may reach another device: no remote copies, remote signals or barrier semaphores. Data moves between devices by JAX's collectives and lax.ppermute only.
A program may use at most 64 MiB of HBM per device.

v0:
```python
import jax
import jax.numpy as jnp
from jax import lax
from jax.sharding import PartitionSpec as P

GH = 8


def passed_along(value, axis, steps):
    count = lax.axis_size(axis)
    pairs = [(source, (source + steps) % count) for source in range(count)]
    return lax.ppermute(value, axis, pairs)


def widen(volume_tile):
    zero_col = jnp.zeros(volume_tile.shape[:3] + (1,), volume_tile.dtype)
    left_shift = jnp.concatenate([zero_col, volume_tile[..., :-1]], 3)
    right_shift = jnp.concatenate([volume_tile[..., 1:], zero_col], 3)
    return jnp.concatenate([left_shift, volume_tile, right_shift], 0)


def tile_border(volume_tile, above, below, front, back):
    tile_count = lax.axis_size("space")
    position = (lax.axis_index("space") + GH + GH // 4) % tile_count
    tile_row = position % GH
    depth_tile = position // GH
    grid_depth = tile_count // GH
    above_rim = above(volume_tile[:, :, -1:, :])
    below_rim = below(volume_tile[:, :, :1, :])
    above_rim = jnp.where(tile_row > 0, above_rim, jnp.zeros_like(above_rim))
    below_rim = jnp.where(tile_row < GH - 1, below_rim, jnp.zeros_like(below_rim))
    taller = jnp.concatenate([above_rim, volume_tile, below_rim], 2)
    front_rim = front(taller[:, -1:])
    back_rim = back(taller[:, :1])
    front_rim = jnp.where(depth_tile > 0, front_rim, jnp.zeros_like(front_rim))
    back_rim = jnp.where(depth_tile < grid_depth - 1, back_rim, jnp.zeros_like(back_rim))
    return jnp.concatenate([front_rim, taller, back_rim], 1)


def input_above(rim_cells):
    return passed_along(rim_cells, "space", 1)


def input_below(rim_cells):
    return passed_along(rim_cells, "space", -1)


def input_front(rim_cells):
    return passed_along(rim_cells, "space", GH)


def input_back(rim_cells):
    return passed_along(rim_cells, "space", -GH)


def hidden_above(rim_cells):
    return passed_along(rim_cells, "space", 1)


def hidden_below(rim_cells):
    return passed_along(rim_cells, "space", -1)


def hidden_front(rim_cells):
    return passed_along(rim_cells, "space", GH)


def hidden_back(rim_cells):
    return passed_along(rim_cells, "space", -GH)


def correlate(stacked, filters, depth_rows, height_rows):
    out_count = filters.shape[3]
    running = jnp.zeros((out_count, depth_rows, height_rows, stacked.shape[3]), jnp.float32)
    for depth_tap in range(3):
        for height_tap in range(3):
            matrix = filters[depth_tap, height_tap].transpose(1, 0, 2).reshape(out_count, -1)
            window = stacked[
                :, depth_tap : depth_tap + depth_rows, height_tap : height_tap + height_rows, :
            ]
            running = running + jnp.einsum(
                "ok,kdhw->odhw", matrix, window, preferred_element_type=jnp.float32
            )
    return running


def local(voxels, first_filters, second_filters):
    depth_rows = voxels.shape[1]
    height_rows = voxels.shape[2]
    padded = tile_border(voxels, input_above, input_below, input_front, input_back)
    hidden = jax.nn.relu(correlate(widen(padded), first_filters, depth_rows, height_rows)).astype(
        jnp.bfloat16
    )
    hidden_pad = tile_border(hidden, hidden_above, hidden_below, hidden_front, hidden_back)
    summed = correlate(
        widen(lax.all_gather(hidden_pad, "chan", axis=0, tiled=True)),
        second_filters,
        depth_rows,
        height_rows,
    )
    return jax.nn.relu(summed).astype(jnp.bfloat16)


def solution(mesh):
    return jax.shard_map(
        local,
        mesh=mesh,
        in_specs=(
            P(None, "space", None, None),
            P(None, None, None, "chan", None),
            P(None, None, None, "chan", None),
        ),
        out_specs=P("chan", "space", None, None),
        check_vma=False,
    )
```

profile of v0, /device:TPU:1, one launch (start us, length us, event | category | flops | bytes accessed | tf_op | source)
XLA Modules:
  0.0 173.7 jit_solution(5258099566370104163)
XLA Ops:
  6.5 1.8 %copy.26 = bf16[32,2,16,512]{3,0,2,1:T(8,128)(2,1)S(1)} copy(bf16[32,2,16,512]{3,2,1,0:T(8,128)(2,1)} %param.3) | data formatting | bytes 2097152 | tf_op args[0]
  8.4 3.9 %collective-permute-start = (bf16[32,2,1,512]{3,0,2,1:T(8,128)(2,1)S(1)}, bf16[32,2,1,512]{3,0,2,1:T(8,128)(2,1)S(1)}, u32[]{:S(2)}, u32[]{:S(2)}) collective-permute-start(bf16[32,2,1,512]{3,0,2,1:T(8,128)(2,1)S(1)} %get-tuple-element.11), channel_id=1, source_target_pairs={{0,4},{4,8},{8,12},{12,16},{16,20},{20,24},{24,28},{28,32},{32,36}... | collective-permute-start | bytes 196616 | tf_op jit(solution)/shard_map/ppermute | solution.py:12
  12.2 7.8 %collective-permute-start.1 = (bf16[32,2,1,512]{3,0,2,1:T(8,128)(2,1)S(1)}, bf16[32,2,1,512]{3,0,2,1:T(8,128)(2,1)S(1)}, u32[]{:S(2)}, u32[]{:S(2)}) collective-permute-start(bf16[32,2,1,512]{3,0,2,1:T(8,128)(2,1)S(1)} %get-tuple-element.12), channel_id=1, source_target_pairs={{0,252},{4,0},{8,4},{12,8},{16,12},{20,16},{24,20},{28,24},{32,28}... | collective-permute-start | bytes 196616 | tf_op jit(solution)/shard_map/ppermute | solution.py:12
  20.0 1.7 collective-permute-done
  22.5 4.6 %collective-permute-start.3 = (bf16[32,1,18,512]{3,0,2,1:T(8,128)(2,1)S(1)}, bf16[32,1,18,512]{3,0,2,1:T(8,128)(2,1)S(1)}, u32[]{:S(2)}, u32[]{:S(2)}) collective-permute-start(bf16[32,1,18,512]{3,0,2,1:T(8,128)(2,1)S(1)} %get-tuple-element.10), channel_id=1, source_target_pairs={{0,224},{4,228},{8,232},{12,236},{16,240},{20,244},{24,248},{28,25... | collective-permute-start | bytes 1769480 | tf_op jit(solution)/shard_map/ppermute | solution.py:12
  27.1 1.5 slice_bitcast_fusion.17
  40.4 5.7 %collective-permute-done.2 = bf16[32,1,18,512]{3,0,2,1:T(8,128)(2,1)S(1)} collective-permute-done((bf16[32,1,18,512]{3,0,2,1:T(8,128)(2,1)S(1)}, bf16[32,1,18,512]{3,0,2,1:T(8,128)(2,1)S(1)}, u32[]{:S(2)}, u32[]{:S(2)}) %collective-permute-start.2) | collective-permute-done | bytes 589856 | tf_op jit(solution)/shard_map/ppermute | solution.py:12
  46.2 4.0 %collective-permute-done.3 = bf16[32,1,18,512]{3,0,2,1:T(8,128)(2,1)S(1)} collective-permute-done((bf16[32,1,18,512]{3,0,2,1:T(8,128)(2,1)S(1)}, bf16[32,1,18,512]{3,0,2,1:T(8,128)(2,1)S(1)}, u32[]{:S(2)}, u32[]{:S(2)}) %collective-permute-start.3) | collective-permute-done | bytes 589856 | tf_op jit(solution)/shard_map/ppermute | solution.py:12
  50.7 1.6 fusion.129
  52.3 2.9 %fusion.6 = bf16[96,4,18,512]{3,0,2,1:T(8,128)(2,1)S(1)} fusion(bf16[32,4,18,511]{3,0,2,1:T(8,128)(2,1)S(1)} %get-tuple-element.8, bf16[32,4,18,511]{3,0,2,1:T(8,128)(2,1)S(1)} %get-tuple-element.7, bf16[32,1,18,512]{3,0,2,1:T(8,128)(2,1)S(1)} %broadcast_select_fusion, bf16[32,2,1,512]{3,0,2,1:T(8,128)(2,1)S(1)} %broadcast_select_fusion.4, ...), kind=kLoop, calls=%fused_computation.10 | loop fusion | flops 63700992 | bytes 14146560 | tf_op jit(solution)/shard_map/concatenate | solution.py:19
  60.2 4.0 %collective-permute-start.4 = (bf16[16,2,1,512]{3,0,2,1:T(8,128)(2,1)S(1)}, bf16[16,2,1,512]{3,0,2,1:T(8,128)(2,1)S(1)}, u32[]{:S(2)}, u32[]{:S(2)}) collective-permute-start(bf16[16,2,1,512]{3,0,2,1:T(8,128)(2,1)S(1)} %get-tuple-element.15), channel_id=1, source_target_pairs={{0,4},{4,8},{8,12},{12,16},{16,20},{20,24},{24,28},{28,32},{32,36}... | collective-permute-start | bytes 98312 | tf_op jit(solution)/shard_map/ppermute | solution.py:12
  64.1 4.5 %collective-permute-start.5 = (bf16[16,2,1,512]{3,0,2,1:T(8,128)(2,1)S(1)}, bf16[16,2,1,512]{3,0,2,1:T(8,128)(2,1)S(1)}, u32[]{:S(2)}, u32[]{:S(2)}) collective-permute-start(bf16[16,2,1,512]{3,0,2,1:T(8,128)(2,1)S(1)} %get-tuple-element.16), channel_id=1, source_target_pairs={{0,252},{4,0},{8,4},{12,8},{16,12},{20,16},{24,20},{28,24},{32,28}... | collective-permute-start | bytes 98312 | tf_op jit(solution)/shard_map/ppermute | solution.py:12
  68.6 1.0 collective-permute-done.4
  69.9 5.1 %collective-permute-start.7 = (bf16[16,1,18,512]{3,0,2,1:T(8,128)(2,1)S(1)}, bf16[16,1,18,512]{3,0,2,1:T(8,128)(2,1)S(1)}, u32[]{:S(2)}, u32[]{:S(2)}) collective-permute-start(bf16[16,1,18,512]{3,0,2,1:T(8,128)(2,1)S(1)} %get-tuple-element.14), channel_id=1, source_target_pairs={{0,224},{4,228},{8,232},{12,236},{16,240},{20,244},{24,248},{28,25... | collective-permute-start | bytes 884744 | tf_op jit(solution)/shard_map/ppermute | solution.py:12
  75.0 4.2 %collective-permute-done.6 = bf16[16,1,18,512]{3,0,2,1:T(8,128)(2,1)S(1)} collective-permute-done((bf16[16,1,18,512]{3,0,2,1:T(8,128)(2,1)S(1)}, bf16[16,1,18,512]{3,0,2,1:T(8,128)(2,1)S(1)}, u32[]{:S(2)}, u32[]{:S(2)}) %collective-permute-start.6) | collective-permute-done | bytes 294944 | tf_op jit(solution)/shard_map/ppermute | solution.py:12
  79.2 5.5 %collective-permute-done.7 = bf16[16,1,18,512]{3,0,2,1:T(8,128)(2,1)S(1)} collective-permute-done((bf16[16,1,18,512]{3,0,2,1:T(8,128)(2,1)S(1)}, bf16[16,1,18,512]{3,0,2,1:T(8,128)(2,1)S(1)}, u32[]{:S(2)}, u32[]{:S(2)}) %collective-permute-start.7) | collective-permute-done | bytes 294944 | tf_op jit(solution)/shard_map/ppermute | solution.py:12
  84.8 1.2 pad_maximum_fusion.2
  86.9 54.6 %all-gather.2.cloned.1.call-done = bf16[64,4,18,512]{3,0,2,1:T(8,128)(2,1)} async-done(((bf16[16,4,18,512]{3,0,2,1:T(8,128)(2,1)}), bf16[64,4,18,512]{3,0,2,1:T(8,128)(2,1)}) %all-gather.2.cloned.1.call-update) | async-done | bytes 4718608 | tf_op jit(solution)/shard_map/all_gather | solution.py:96
  141.6 9.0 %fusion.128 = (bf16[64,4,18,511]{3,0,2,1:T(8,128)(2,1)S(1)}, bf16[64,4,18,511]{3,0,2,1:T(8,128)(2,1)}) fusion(bf16[64,4,18,512]{3,0,2,1:T(8,128)(2,1)} %all-gather.2.cloned.1.call-done), kind=kLoop, calls=%fused_computation.118 | loop fusion | bytes 18837504 | tf_op jit(solution)/shard_map/slice | solution.py:17
  150.6 6.7 %fusion.2 = bf16[192,4,18,512]{3,0,2,1:T(8,128)(2,1)S(1)} fusion(bf16[64,4,18,511]{3,0,2,1:T(8,128)(2,1)} %get-tuple-element.6, bf16[64,4,18,511]{3,0,2,1:T(8,128)(2,1)S(1)} %get-tuple-element.5, bf16[64,4,18,512]{3,0,2,1:T(8,128)(2,1)S(1)} %copy-done), kind=kLoop, calls=%fused_computation.4 | loop fusion | flops 70778880 | bytes 28293120 | tf_op jit(solution)/shard_map/concatenate | solution.py:19
  158.2 0.9 fusion.59
  162.0 0.9 fusion.71
  164.8 0.9 fusion.107
  165.7 1.1 copy.47
  (95 shorter events, 24.8 us)
Async XLA Ops:
  6.5 135.0 %all-gather.2.cloned.1.call-start = ((), (), s32[]{:S(2)}) async-start(), calls=%async_computation | async-start | bytes 5898240 | tf_op jit(solution)/shard_map/all_gather | solution.py:96
  8.4 13.3 %collective-permute-start = (bf16[32,2,1,512]{3,0,2,1:T(8,128)(2,1)S(1)}, bf16[32,2,1,512]{3,0,2,1:T(8,128)(2,1)S(1)}, u32[]{:S(2)}, u32[]{:S(2)}) collective-permute-start(bf16[32,2,1,512]{3,0,2,1:T(8,128)(2,1)S(1)} %get-tuple-element.11), channel_id=1, source_target_pairs={{0,4},{4,8},{8,12},{12,16},{16,20},{20,24},{24,28},{28,32},{32,36}... | collective-permute-start | bytes 196616 | tf_op jit(solution)/shard_map/ppermute | solution.py:12
  12.2 9.4 %collective-permute-start.1 = (bf16[32,2,1,512]{3,0,2,1:T(8,128)(2,1)S(1)}, bf16[32,2,1,512]{3,0,2,1:T(8,128)(2,1)S(1)}, u32[]{:S(2)}, u32[]{:S(2)}) collective-permute-start(bf16[32,2,1,512]{3,0,2,1:T(8,128)(2,1)S(1)} %get-tuple-element.12), channel_id=1, source_target_pairs={{0,252},{4,0},{8,4},{12,8},{16,12},{20,16},{24,20},{28,24},{32,28}... | collective-permute-start | bytes 196616 | tf_op jit(solution)/shard_map/ppermute | solution.py:12
  22.0 24.2 %collective-permute-start.2 = (bf16[32,1,18,512]{3,0,2,1:T(8,128)(2,1)S(1)}, bf16[32,1,18,512]{3,0,2,1:T(8,128)(2,1)S(1)}, u32[]{:S(2)}, u32[]{:S(2)}) collective-permute-start(bf16[32,1,18,512]{3,0,2,1:T(8,128)(2,1)S(1)} %get-tuple-element.9), channel_id=1, source_target_pairs={{0,32},{4,36},{8,40},{12,44},{16,48},{20,52},{24,56},{28,60},{32,6... | collective-permute-start | bytes 1769480 | tf_op jit(solution)/shard_map/ppermute | solution.py:12
  22.5 27.7 %collective-permute-start.3 = (bf16[32,1,18,512]{3,0,2,1:T(8,128)(2,1)S(1)}, bf16[32,1,18,512]{3,0,2,1:T(8,128)(2,1)S(1)}, u32[]{:S(2)}, u32[]{:S(2)}) collective-permute-start(bf16[32,1,18,512]{3,0,2,1:T(8,128)(2,1)S(1)} %get-tuple-element.10), channel_id=1, source_target_pairs={{0,224},{4,228},{8,232},{12,236},{16,240},{20,244},{24,248},{28,25... | collective-permute-start | bytes 1769480 | tf_op jit(solution)/shard_map/ppermute | solution.py:12
  52.3 2.9 %copy-start.2 = (bf16[16,96,1,1]{1,0,2,3:T(8,128)(2,1)S(1)}, bf16[16,96,1,1]{1,0,2,3:T(8,128)(2,1)}, u32[]{:S(2)}) copy-start(bf16[16,96,1,1]{1,0,2,3:T(8,128)(2,1)} %reshape.80) | copy-start | bytes 9220
  52.3 3.5 %copy-start.3 = (bf16[16,96,1,1]{1,0,2,3:T(8,128)(2,1)S(1)}, bf16[16,96,1,1]{1,0,2,3:T(8,128)(2,1)}, u32[]{:S(2)}) copy-start(bf16[16,96,1,1]{1,0,2,3:T(8,128)(2,1)} %reshape.79) | copy-start | bytes 9220
  55.2 1.1 copy-start.4
  55.2 1.6 copy-start.5
  55.8 1.6 copy-start.6
  56.3 1.6 copy-start.7
  56.8 1.6 copy-start.8
  57.4 1.6 copy-start.9
  57.9 1.6 copy-start.10
  59.5 26.5 %copy-start.1 = (bf16[3,3,3,16,64]{4,3,2,1,0:T(8,128)(2,1)S(1)}, bf16[3,3,3,16,64]{4,3,2,1,0:T(8,128)(2,1)}, u32[]{:S(2)}) copy-start(bf16[3,3,3,16,64]{4,3,2,1,0:T(8,128)(2,1)} %param.5) | copy-start | bytes 165892
  60.2 9.5 %collective-permute-start.4 = (bf16[16,2,1,512]{3,0,2,1:T(8,128)(2,1)S(1)}, bf16[16,2,1,512]{3,0,2,1:T(8,128)(2,1)S(1)}, u32[]{:S(2)}, u32[]{:S(2)}) collective-permute-start(bf16[16,2,1,512]{3,0,2,1:T(8,128)(2,1)S(1)} %get-tuple-element.15), channel_id=1, source_target_pairs={{0,4},{4,8},{8,12},{12,16},{16,20},{20,24},{24,28},{28,32},{32,36}... | collective-permute-start | bytes 98312 | tf_op jit(solution)/shard_map/ppermute | solution.py:12
  64.1 5.6 %collective-permute-start.5 = (bf16[16,2,1,512]{3,0,2,1:T(8,128)(2,1)S(1)}, bf16[16,2,1,512]{3,0,2,1:T(8,128)(2,1)S(1)}, u32[]{:S(2)}, u32[]{:S(2)}) collective-permute-start(bf16[16,2,1,512]{3,0,2,1:T(8,128)(2,1)S(1)} %get-tuple-element.16), channel_id=1, source_target_pairs={{0,252},{4,0},{8,4},{12,8},{16,12},{20,16},{24,20},{28,24},{32,28}... | collective-permute-start | bytes 98312 | tf_op jit(solution)/shard_map/ppermute | solution.py:12
  69.8 9.4 %collective-permute-start.6 = (bf16[16,1,18,512]{3,0,2,1:T(8,128)(2,1)S(1)}, bf16[16,1,18,512]{3,0,2,1:T(8,128)(2,1)S(1)}, u32[]{:S(2)}, u32[]{:S(2)}) collective-permute-start(bf16[16,1,18,512]{3,0,2,1:T(8,128)(2,1)S(1)} %get-tuple-element.13), channel_id=1, source_target_pairs={{0,32},{4,36},{8,40},{12,44},{16,48},{20,52},{24,56},{28,60},{32,6... | collective-permute-start | bytes 884744 | tf_op jit(solution)/shard_map/ppermute | solution.py:12
  69.9 14.8 %collective-permute-start.7 = (bf16[16,1,18,512]{3,0,2,1:T(8,128)(2,1)S(1)}, bf16[16,1,18,512]{3,0,2,1:T(8,128)(2,1)S(1)}, u32[]{:S(2)}, u32[]{:S(2)}) collective-permute-start(bf16[16,1,18,512]{3,0,2,1:T(8,128)(2,1)S(1)} %get-tuple-element.14), channel_id=1, source_target_pairs={{0,224},{4,228},{8,232},{12,236},{16,240},{20,244},{24,248},{28,25... | collective-permute-start | bytes 884744 | tf_op jit(solution)/shard_map/ppermute | solution.py:12
  141.6 9.1 %copy-start = (bf16[64,4,18,512]{3,0,2,1:T(8,128)(2,1)S(1)}, bf16[64,4,18,512]{3,0,2,1:T(8,128)(2,1)}, u32[]{:S(2)}) copy-start(bf16[64,4,18,512]{3,0,2,1:T(8,128)(2,1)} %all-gather.2.cloned.1.call-done) | copy-start | bytes 14155780
Sparse Core Ops, SparseCore 0:
  86.1 55.3 all-gather.1
where the time goes:
time: 174 us
  waiting for transfers between devices  76.8 us (44%)
  starting transfers between devices  30.5 us (18%)
  local copies, waits for them, and re-layouts  27.9 us (16%)
  between operations  13.6 us (8%)
  matrix products  13.3 us (8%)
  other arithmetic  11.6 us (7%)
    all_gather x1, waiting for transfers between devices, local(): lax.all_gather(hidden_pad, 'chan', axis=0, tiled=True)  54.6 us
    ppermute x8, starting transfers between devices, passed_along(): return lax.ppermute(value, axis, pairs)  30.4 us
    ppermute x8, waiting for transfers between devices, passed_along(): return lax.ppermute(value, axis, pairs)  22.2 us
    dot_general x18, matrix products, correlate(): jnp.einsum('ok,kdhw->odhw', matrix, window, preferred_element_type=jnp.fl...  13.3 us
    slice x2, local copies, waits for them, and re-layouts, widen(): left_shift = jnp.concatenate([zero_col, volume_tile[..., :-1]], 3)  10.6 us
    concatenate x2, other arithmetic, widen(): return jnp.concatenate([left_shift, volume_tile, right_shift], 0)  9.59 us
    transpose x20, local copies, waits for them, and re-layouts, correlate(): filters[depth_tap, height_tap].transpose(1, 0, 2).reshape(out_count, -1)  7.27 us
    reshape x18, local copies, waits for them, and re-layouts, correlate(): filters[depth_tap, height_tap].transpose(1, 0, 2).reshape(out_count, -1)  6.94 us
  transfers between devices with their start and end apart: 9, of which 7 were waited for; matrix products, arithmetic and copies ran while one was open for 8% of the time, Pallas kernels for 0%

commit v1 on v0

--- a/solution.py
+++ b/solution.py
@@ -93,7 +93,12 @@
     )
     hidden_pad = tile_border(hidden, hidden_above, hidden_below, hidden_front, hidden_back)
     summed = correlate(
-        widen(lax.all_gather(hidden_pad, "chan", axis=0, tiled=True)),
+        widen(
+            jnp.concatenate(
+                lax.all_to_all(jnp.stack([hidden_pad] * lax.axis_size("chan")), "chan", 0, 0),
+                axis=0,
+            )
+        ),
         second_filters,
         depth_rows,
         height_rows,

time: 174 us -> 167 us (0.960)
  between operations: 13.6 us -> 0.26 us
  starting transfers between devices: 30.5 us -> 37.9 us
  waiting for transfers between devices: 76.8 us -> 74 us
  local copies, waits for them, and re-layouts: 27.9 us -> 30.2 us
    all_gather x1 -> x0, waiting for transfers between devices: 54.6 us -> none  [local(): lax.all_gather(hidden_pad, 'chan', axis=0, tiled=True)]
    all_to_all x0 -> x1, waiting for transfers between devices: none -> 51.6 us  [local(): lax.all_to_all(jnp.stack([hidden_pad] * lax.axis_size('chan')), 'chan', 0...]
    all_to_all x0 -> x1, starting transfers between devices: none -> 7.44 us  [local(): lax.all_to_all(jnp.stack([hidden_pad] * lax.axis_size('chan')), 'chan', 0...]
    slice x2, local copies, waits for them, and re-layouts: 10.6 us -> 7.23 us  [widen(): left_shift = jnp.concatenate([zero_col, volume_tile[..., :-1]], 3)]
    all_to_all x0 -> x1, local copies, waits for them, and re-layouts: none -> 2.86 us  [local(): lax.all_to_all(jnp.stack([hidden_pad] * lax.axis_size('chan')), 'chan', 0...]
    another operation x0 -> x1, local copies, waits for them, and re-layouts: none -> 2.83 us  [local(): jnp.stack([hidden_pad] * lax.axis_size('chan'))]
  transfers between devices with their start and end apart: 9 -> 9, of which waited for: 7 -> 7; matrix products, arithmetic and copies ran while one was open for 8% -> 9% of each run, Pallas kernels for 0% -> 0%
where the time goes in v1:
time: 167 us; the launch traced here: 166 us
  waiting for transfers between devices  74 us (44%)
  starting transfers between devices  37.9 us (23%)
  local copies, waits for them, and re-layouts  30.2 us (18%)
  matrix products  13.3 us (8%)
  other arithmetic  10.6 us (6%)
    all_to_all x1, waiting for transfers between devices, local(): lax.all_to_all(jnp.stack([hidden_pad] * lax.axis_size('chan')), 'chan', 0...  51.6 us
    ppermute x8, starting transfers between devices, passed_along(): return lax.ppermute(value, axis, pairs)  30.4 us
    ppermute x8, waiting for transfers between devices, passed_along(): return lax.ppermute(value, axis, pairs)  22.4 us
    dot_general x18, matrix products, correlate(): jnp.einsum('ok,kdhw->odhw', matrix, window, preferred_element_type=jnp.fl...  13.3 us
    concatenate x2, other arithmetic, widen(): return jnp.concatenate([left_shift, volume_tile, right_shift], 0)  9.59 us
    all_to_all x1, starting transfers between devices, local(): lax.all_to_all(jnp.stack([hidden_pad] * lax.axis_size('chan')), 'chan', 0...  7.44 us
    transpose x20, local copies, waits for them, and re-layouts, correlate(): filters[depth_tap, height_tap].transpose(1, 0, 2).reshape(out_count, -1)  7.26 us
    slice x2, local copies, waits for them, and re-layouts, widen(): left_shift = jnp.concatenate([zero_col, volume_tile[..., :-1]], 3)  7.23 us
  transfers between devices with their start and end apart: 9, of which 7 were waited for; matrix products, arithmetic and copies ran while one was open for 9% of the time, Pallas kernels for 0%

profile of v1, /device:TPU:1, one launch (start us, length us, event | category | flops | bytes accessed | tf_op | source)
XLA Modules:
  0.0 166.1 jit_solution(13487228163857779144)
XLA Ops:
  0.0 1.8 %copy.48 = bf16[32,2,16,512]{3,0,2,1:T(8,128)(2,1)S(1)} copy(bf16[32,2,16,512]{3,2,1,0:T(8,128)(2,1)} %param.3) | data formatting | bytes 2097152 | tf_op args[0]
  1.8 3.9 %collective-permute-start = (bf16[32,2,1,512]{3,0,2,1:T(8,128)(2,1)S(1)}, bf16[32,2,1,512]{3,0,2,1:T(8,128)(2,1)S(1)}, u32[]{:S(2)}, u32[]{:S(2)}) collective-permute-start(bf16[32,2,1,512]{3,0,2,1:T(8,128)(2,1)S(1)} %get-tuple-element.11), channel_id=1, source_target_pairs={{0,4},{4,8},{8,12},{12,16},{16,20},{20,24},{24,28},{28,32},{32,36}... | collective-permute-start | bytes 196616 | tf_op jit(solution)/shard_map/ppermute | solution.py:12
  5.7 7.8 %collective-permute-start.1 = (bf16[32,2,1,512]{3,0,2,1:T(8,128)(2,1)S(1)}, bf16[32,2,1,512]{3,0,2,1:T(8,128)(2,1)S(1)}, u32[]{:S(2)}, u32[]{:S(2)}) collective-permute-start(bf16[32,2,1,512]{3,0,2,1:T(8,128)(2,1)S(1)} %get-tuple-element.12), channel_id=1, source_target_pairs={{0,252},{4,0},{8,4},{12,8},{16,12},{20,16},{24,20},{28,24},{32,28}... | collective-permute-start | bytes 196616 | tf_op jit(solution)/shard_map/ppermute | solution.py:12
  13.5 1.7 %collective-permute-done = bf16[32,2,1,512]{3,0,2,1:T(8,128)(2,1)S(1)} collective-permute-done((bf16[32,2,1,512]{3,0,2,1:T(8,128)(2,1)S(1)}, bf16[32,2,1,512]{3,0,2,1:T(8,128)(2,1)S(1)}, u32[]{:S(2)}, u32[]{:S(2)}) %collective-permute-start) | collective-permute-done | bytes 65568 | tf_op jit(solution)/shard_map/ppermute | solution.py:12
  16.0 4.6 %collective-permute-start.3 = (bf16[32,1,18,512]{3,0,2,1:T(8,128)(2,1)S(1)}, bf16[32,1,18,512]{3,0,2,1:T(8,128)(2,1)S(1)}, u32[]{:S(2)}, u32[]{:S(2)}) collective-permute-start(bf16[32,1,18,512]{3,0,2,1:T(8,128)(2,1)S(1)} %get-tuple-element.10), channel_id=1, source_target_pairs={{0,224},{4,228},{8,232},{12,236},{16,240},{20,244},{24,248},{28,25... | collective-permute-start | bytes 1769480 | tf_op jit(solution)/shard_map/ppermute | solution.py:12
  20.6 1.5 slice_bitcast_fusion.17
  33.9 5.7 %collective-permute-done.2 = bf16[32,1,18,512]{3,0,2,1:T(8,128)(2,1)S(1)} collective-permute-done((bf16[32,1,18,512]{3,0,2,1:T(8,128)(2,1)S(1)}, bf16[32,1,18,512]{3,0,2,1:T(8,128)(2,1)S(1)}, u32[]{:S(2)}, u32[]{:S(2)}) %collective-permute-start.2) | collective-permute-done | bytes 589856 | tf_op jit(solution)/shard_map/ppermute | solution.py:12
  39.7 4.0 %collective-permute-done.3 = bf16[32,1,18,512]{3,0,2,1:T(8,128)(2,1)S(1)} collective-permute-done((bf16[32,1,18,512]{3,0,2,1:T(8,128)(2,1)S(1)}, bf16[32,1,18,512]{3,0,2,1:T(8,128)(2,1)S(1)}, u32[]{:S(2)}, u32[]{:S(2)}) %collective-permute-start.3) | collective-permute-done | bytes 589856 | tf_op jit(solution)/shard_map/ppermute | solution.py:12
  44.1 1.6 fusion.129
  45.7 2.9 %fusion.6 = bf16[96,4,18,512]{3,0,2,1:T(8,128)(2,1)S(1)} fusion(bf16[32,4,18,511]{3,0,2,1:T(8,128)(2,1)S(1)} %get-tuple-element.8, bf16[32,4,18,511]{3,0,2,1:T(8,128)(2,1)S(1)} %get-tuple-element.7, bf16[32,1,18,512]{3,0,2,1:T(8,128)(2,1)S(1)} %broadcast_select_fusion, bf16[32,2,1,512]{3,0,2,1:T(8,128)(2,1)S(1)} %broadcast_select_fusion.4, ...), kind=kLoop, calls=%fused_computation.10 | loop fusion | flops 63700992 | bytes 14146560 | tf_op jit(solution)/shard_map/concatenate | solution.py:19
  53.6 4.0 %collective-permute-start.4 = (bf16[16,2,1,512]{3,0,2,1:T(8,128)(2,1)S(1)}, bf16[16,2,1,512]{3,0,2,1:T(8,128)(2,1)S(1)}, u32[]{:S(2)}, u32[]{:S(2)}) collective-permute-start(bf16[16,2,1,512]{3,0,2,1:T(8,128)(2,1)S(1)} %get-tuple-element.15), channel_id=1, source_target_pairs={{0,4},{4,8},{8,12},{12,16},{16,20},{20,24},{24,28},{28,32},{32,36}... | collective-permute-start | bytes 98312 | tf_op jit(solution)/shard_map/ppermute | solution.py:12
  57.6 4.3 %collective-permute-start.5 = (bf16[16,2,1,512]{3,0,2,1:T(8,128)(2,1)S(1)}, bf16[16,2,1,512]{3,0,2,1:T(8,128)(2,1)S(1)}, u32[]{:S(2)}, u32[]{:S(2)}) collective-permute-start(bf16[16,2,1,512]{3,0,2,1:T(8,128)(2,1)S(1)} %get-tuple-element.16), channel_id=1, source_target_pairs={{0,252},{4,0},{8,4},{12,8},{16,12},{20,16},{24,20},{28,24},{32,28}... | collective-permute-start | bytes 98312 | tf_op jit(solution)/shard_map/ppermute | solution.py:12
  61.9 1.2 collective-permute-done.4
  63.6 5.1 %collective-permute-start.7 = (bf16[16,1,18,512]{3,0,2,1:T(8,128)(2,1)S(1)}, bf16[16,1,18,512]{3,0,2,1:T(8,128)(2,1)S(1)}, u32[]{:S(2)}, u32[]{:S(2)}) collective-permute-start(bf16[16,1,18,512]{3,0,2,1:T(8,128)(2,1)S(1)} %get-tuple-element.14), channel_id=1, source_target_pairs={{0,224},{4,228},{8,232},{12,236},{16,240},{20,244},{24,248},{28,25... | collective-permute-start | bytes 884744 | tf_op jit(solution)/shard_map/ppermute | solution.py:12
  68.6 4.2 %collective-permute-done.6 = bf16[16,1,18,512]{3,0,2,1:T(8,128)(2,1)S(1)} collective-permute-done((bf16[16,1,18,512]{3,0,2,1:T(8,128)(2,1)S(1)}, bf16[16,1,18,512]{3,0,2,1:T(8,128)(2,1)S(1)}, u32[]{:S(2)}, u32[]{:S(2)}) %collective-permute-start.6) | collective-permute-done | bytes 294944 | tf_op jit(solution)/shard_map/ppermute | solution.py:12
  72.9 5.5 %collective-permute-done.7 = bf16[16,1,18,512]{3,0,2,1:T(8,128)(2,1)S(1)} collective-permute-done((bf16[16,1,18,512]{3,0,2,1:T(8,128)(2,1)S(1)}, bf16[16,1,18,512]{3,0,2,1:T(8,128)(2,1)S(1)}, u32[]{:S(2)}, u32[]{:S(2)}) %collective-permute-start.7) | collective-permute-done | bytes 294944 | tf_op jit(solution)/shard_map/ppermute | solution.py:12
  78.6 2.8 %stack.2 = bf16[4,16,4,18,512]{4,1,3,2,0:T(8,128)(2,1)} broadcast(bf16[16,4,18,512]{3,0,2,1:T(8,128)(2,1)S(1)} %pad_maximum_fusion.2), dimensions={1,2,3,4} | broadcast | bytes 5898240 | tf_op jit(solution)/shard_map/stack | solution.py:98
  81.4 7.4 %all-to-all-start = ((bf16[4,16,4,18,512]{4,1,3,2,0:T(8,128)(2,1)}), bf16[4,16,4,18,512]{4,1,3,2,0:T(8,128)(2,1)}, u32[]{:S(2)}, u32[]{:S(2)}) async-start(bf16[4,16,4,18,512]{4,1,3,2,0:T(8,128)(2,1)} %stack.2), calls=%async_computation | async-start | bytes 9437184 | tf_op jit(solution)/shard_map/all_to_all | solution.py:98
  89.8 51.6 %all-to-all-done = bf16[4,16,4,18,512]{4,1,3,2,0:T(8,128)(2,1)} async-done(((bf16[4,16,4,18,512]{4,1,3,2,0:T(8,128)(2,1)}), bf16[4,16,4,18,512]{4,1,3,2,0:T(8,128)(2,1)}, u32[]{:S(2)}, u32[]{:S(2)}) %all-to-all-start) | async-done | bytes 4718624 | tf_op jit(solution)/shard_map/all_to_all | solution.py:98
  141.4 2.9 %copy.60 = bf16[4,16,4,18,512]{4,1,0,3,2:T(8,128)(2,1)S(1)} copy(bf16[4,16,4,18,512]{4,1,3,2,0:T(8,128)(2,1)} %all-to-all-done) | data formatting | bytes 9437184 | tf_op jit(solution)/shard_map/all_to_all | solution.py:98
  144.3 5.7 %fusion.128 = (bf16[64,4,18,511]{3,0,2,1:T(8,128)(2,1)S(1)}, bf16[64,4,18,511]{3,0,2,1:T(8,128)(2,1)}) fusion(bf16[64,4,18,512]{3,0,2,1:T(8,128)(2,1)S(1)} %bitcast.131), kind=kLoop, calls=%fused_computation.118 | loop fusion | bytes 18837504 | tf_op jit(solution)/shard_map/slice | solution.py:17
  149.9 6.7 %fusion.2 = bf16[192,4,18,512]{3,0,2,1:T(8,128)(2,1)S(1)} fusion(bf16[64,4,18,511]{3,0,2,1:T(8,128)(2,1)} %get-tuple-element.6, bf16[64,4,18,511]{3,0,2,1:T(8,128)(2,1)S(1)} %get-tuple-element.5, bf16[64,4,18,512]{3,0,2,1:T(8,128)(2,1)S(1)} %bitcast.132), kind=kLoop, calls=%fused_computation.4 | loop fusion | flops 70778880 | bytes 28293120 | tf_op jit(solution)/shard_map/concatenate | solution.py:19
  164.1 0.9 fusion.107
  165.0 1.1 copy.70
  (94 shorter events, 27.0 us)
Async XLA Ops:
  1.8 13.3 %collective-permute-start = (bf16[32,2,1,512]{3,0,2,1:T(8,128)(2,1)S(1)}, bf16[32,2,1,512]{3,0,2,1:T(8,128)(2,1)S(1)}, u32[]{:S(2)}, u32[]{:S(2)}) collective-permute-start(bf16[32,2,1,512]{3,0,2,1:T(8,128)(2,1)S(1)} %get-tuple-element.11), channel_id=1, source_target_pairs={{0,4},{4,8},{8,12},{12,16},{16,20},{20,24},{24,28},{28,32},{32,36}... | collective-permute-start | bytes 196616 | tf_op jit(solution)/shard_map/ppermute | solution.py:12
  5.7 9.4 %collective-permute-start.1 = (bf16[32,2,1,512]{3,0,2,1:T(8,128)(2,1)S(1)}, bf16[32,2,1,512]{3,0,2,1:T(8,128)(2,1)S(1)}, u32[]{:S(2)}, u32[]{:S(2)}) collective-permute-start(bf16[32,2,1,512]{3,0,2,1:T(8,128)(2,1)S(1)} %get-tuple-element.12), channel_id=1, source_target_pairs={{0,252},{4,0},{8,4},{12,8},{16,12},{20,16},{24,20},{28,24},{32,28}... | collective-permute-start | bytes 196616 | tf_op jit(solution)/shard_map/ppermute | solution.py:12
  15.4 24.2 %collective-permute-start.2 = (bf16[32,1,18,512]{3,0,2,1:T(8,128)(2,1)S(1)}, bf16[32,1,18,512]{3,0,2,1:T(8,128)(2,1)S(1)}, u32[]{:S(2)}, u32[]{:S(2)}) collective-permute-start(bf16[32,1,18,512]{3,0,2,1:T(8,128)(2,1)S(1)} %get-tuple-element.9), channel_id=1, source_target_pairs={{0,32},{4,36},{8,40},{12,44},{16,48},{20,52},{24,56},{28,60},{32,6... | collective-permute-start | bytes 1769480 | tf_op jit(solution)/shard_map/ppermute | solution.py:12
  16.0 27.7 %collective-permute-start.3 = (bf16[32,1,18,512]{3,0,2,1:T(8,128)(2,1)S(1)}, bf16[32,1,18,512]{3,0,2,1:T(8,128)(2,1)S(1)}, u32[]{:S(2)}, u32[]{:S(2)}) collective-permute-start(bf16[32,1,18,512]{3,0,2,1:T(8,128)(2,1)S(1)} %get-tuple-element.10), channel_id=1, source_target_pairs={{0,224},{4,228},{8,232},{12,236},{16,240},{20,244},{24,248},{28,25... | collective-permute-start | bytes 1769480 | tf_op jit(solution)/shard_map/ppermute | solution.py:12
  45.7 2.9 %copy-start.1 = (bf16[16,96,1,1]{1,0,2,3:T(8,128)(2,1)S(1)}, bf16[16,96,1,1]{1,0,2,3:T(8,128)(2,1)}, u32[]{:S(2)}) copy-start(bf16[16,96,1,1]{1,0,2,3:T(8,128)(2,1)} %reshape.86) | copy-start | bytes 9220
  45.7 3.5 %copy-start.2 = (bf16[16,96,1,1]{1,0,2,3:T(8,128)(2,1)S(1)}, bf16[16,96,1,1]{1,0,2,3:T(8,128)(2,1)}, u32[]{:S(2)}) copy-start(bf16[16,96,1,1]{1,0,2,3:T(8,128)(2,1)} %reshape.85) | copy-start | bytes 9220
  48.7 1.1 copy-start.3
  48.7 1.6 copy-start.4
  49.2 1.6 copy-start.5
  49.8 1.6 copy-start.6
  50.3 1.6 copy-start.7
  50.8 1.6 copy-start.8
  51.4 1.6 copy-start.9
  53.6 9.5 %collective-permute-start.4 = (bf16[16,2,1,512]{3,0,2,1:T(8,128)(2,1)S(1)}, bf16[16,2,1,512]{3,0,2,1:T(8,128)(2,1)S(1)}, u32[]{:S(2)}, u32[]{:S(2)}) collective-permute-start(bf16[16,2,1,512]{3,0,2,1:T(8,128)(2,1)S(1)} %get-tuple-element.15), channel_id=1, source_target_pairs={{0,4},{4,8},{8,12},{12,16},{16,20},{20,24},{24,28},{28,32},{32,36}... | collective-permute-start | bytes 98312 | tf_op jit(solution)/shard_map/ppermute | solution.py:12
  57.6 5.6 %collective-permute-start.5 = (bf16[16,2,1,512]{3,0,2,1:T(8,128)(2,1)S(1)}, bf16[16,2,1,512]{3,0,2,1:T(8,128)(2,1)S(1)}, u32[]{:S(2)}, u32[]{:S(2)}) collective-permute-start(bf16[16,2,1,512]{3,0,2,1:T(8,128)(2,1)S(1)} %get-tuple-element.16), channel_id=1, source_target_pairs={{0,252},{4,0},{8,4},{12,8},{16,12},{20,16},{24,20},{28,24},{32,28}... | collective-permute-start | bytes 98312 | tf_op jit(solution)/shard_map/ppermute | solution.py:12
  63.3 9.5 %collective-permute-start.6 = (bf16[16,1,18,512]{3,0,2,1:T(8,128)(2,1)S(1)}, bf16[16,1,18,512]{3,0,2,1:T(8,128)(2,1)S(1)}, u32[]{:S(2)}, u32[]{:S(2)}) collective-permute-start(bf16[16,1,18,512]{3,0,2,1:T(8,128)(2,1)S(1)} %get-tuple-element.13), channel_id=1, source_target_pairs={{0,32},{4,36},{8,40},{12,44},{16,48},{20,52},{24,56},{28,60},{32,6... | collective-permute-start | bytes 884744 | tf_op jit(solution)/shard_map/ppermute | solution.py:12
  63.6 14.8 %collective-permute-start.7 = (bf16[16,1,18,512]{3,0,2,1:T(8,128)(2,1)S(1)}, bf16[16,1,18,512]{3,0,2,1:T(8,128)(2,1)S(1)}, u32[]{:S(2)}, u32[]{:S(2)}) collective-permute-start(bf16[16,1,18,512]{3,0,2,1:T(8,128)(2,1)S(1)} %get-tuple-element.14), channel_id=1, source_target_pairs={{0,224},{4,228},{8,232},{12,236},{16,240},{20,244},{24,248},{28,25... | collective-permute-start | bytes 884744 | tf_op jit(solution)/shard_map/ppermute | solution.py:12
  78.6 10.3 %copy-start = (bf16[3,3,3,16,64]{4,3,2,1,0:T(8,128)(2,1)S(1)}, bf16[3,3,3,16,64]{4,3,2,1,0:T(8,128)(2,1)}, u32[]{:S(2)}) copy-start(bf16[3,3,3,16,64]{4,3,2,1,0:T(8,128)(2,1)} %param.5) | copy-start | bytes 165892
  81.4 60.0 %all-to-all-start = ((bf16[4,16,4,18,512]{4,1,3,2,0:T(8,128)(2,1)}), bf16[4,16,4,18,512]{4,1,3,2,0:T(8,128)(2,1)}, u32[]{:S(2)}, u32[]{:S(2)}) async-start(bf16[4,16,4,18,512]{4,1,3,2,0:T(8,128)(2,1)} %stack.2), calls=%async_computation | async-start | bytes 9437184 | tf_op jit(solution)/shard_map/all_to_all | solution.py:98
